TPU v7x, 32 devices: a whole 2x2x4 slice. The times are simulated.
32 devices in a mesh: ctx: 8 (over y, x, core), head: 4 (over z).
Axes of the slice: x: 2, y: 2, z: 4, core: 2. Of those that a mesh axis runs over, the one named last changes fastest.
Arguments:
- queries: bfloat16 [4096, 4096], P(('ctx', 'head')), may hold values from -42 to 42
- keys: bfloat16 [4096, 1024], P(('ctx', 'head')), may hold values from -4 to 4
- values: bfloat16 [4096, 1024], P(('ctx', 'head')), may hold values from -6 to 6
- out_grad: bfloat16 [4096, 4096], P(('ctx', 'head')), may hold values from -6 to 6
- beacon_pos: int32 [8, 64], P('ctx'), may hold values from 0 to 511, as said below
Outputs:
- attended: bfloat16 [4096, 4096], P(('ctx', 'head'))
- query_grad: bfloat16 [4096, 4096], P(('ctx', 'head'))
- key_grad: bfloat16 [4096, 1024], P(('ctx', 'head'))
- value_grad: bfloat16 [4096, 1024], P(('ctx', 'head'))
Inputs may be any that keep to these rules, and one draw needn't show every extreme that they name: `beacon_pos`: row c holds 64 distinct positions in increasing order, the first equal to 0 and the last equal to 511.
All inputs are finite; a program needn't handle non-finite values.
Results may differ from a plain program's by a relative error of at most 0.029.
Values may be sent and summed in bfloat16 or wider, within the bound.
No kernel may reach another device: no remote copies, remote signals or barrier semaphores. Data moves between devices by JAX's collectives and lax.ppermute only.
A program may use at most 128 MiB of HBM per device.

v0:
```python
import jax
import jax.numpy as jnp
from jax import lax
from jax.sharding import PartitionSpec as P

HD = 128
NEG_FILL = -1e30


def local(queries, keys, values, out_grad, beacon_pos):
    query_rows, key_rows, value_rows, grad_rows = (
        lax.all_to_all(queries, "head", split_axis=1, concat_axis=0, tiled=True),
        lax.all_to_all(keys, "head", split_axis=1, concat_axis=0, tiled=True),
        lax.all_to_all(values, "head", split_axis=1, concat_axis=0, tiled=True),
        lax.all_to_all(out_grad, "head", split_axis=1, concat_axis=0, tiled=True),
    )
    window = query_rows.shape[0]
    kv_local = key_rows.shape[1] // HD
    group_size = query_rows.shape[1] // HD // kv_local
    scaling = HD ** (-0.5)
    query_head_rows = query_rows.reshape(window, kv_local, group_size, HD)
    head_gradients = grad_rows.reshape(window, kv_local, group_size, HD)
    key_heads = key_rows.reshape(window, kv_local, HD)
    value_heads = value_rows.reshape(window, kv_local, HD)
    positions = beacon_pos[0]
    beacon_keys, beacon_values = (
        lax.all_gather(key_rows[positions], "ctx", axis=0, tiled=True),
        lax.all_gather(value_rows[positions], "ctx", axis=0, tiled=True),
    )
    beacon_total = beacon_keys.shape[0]
    per_shard = positions.shape[0]
    beacon_key_heads = beacon_keys.reshape(beacon_total, kv_local, HD)
    beacon_value_heads = beacon_values.reshape(beacon_total, kv_local, HD)
    owners = jnp.arange(beacon_total, dtype=jnp.int32) // per_shard
    shard_id = lax.axis_index("ctx")
    block_rows = min(beacon_total, 512)
    block_count = beacon_total // block_rows
    causal = jnp.arange(window)[:, None] >= jnp.arange(window)[None, :]
    local_scores = (
        jnp.einsum("wkgd,vkd->kgwv", query_head_rows, key_heads, preferred_element_type=jnp.float32)
        * scaling
    )
    local_scores = jnp.where(causal, local_scores, NEG_FILL)

    def beacon_scores(block_index):
        start = block_index * block_rows
        key_tile_block = lax.dynamic_slice_in_dim(beacon_key_heads, start, block_rows, 0)
        value_tile_block = lax.dynamic_slice_in_dim(beacon_value_heads, start, block_rows, 0)
        seen = lax.dynamic_slice_in_dim(owners, start, block_rows, 0) < shard_id
        scores = (
            jnp.einsum(
                "jahm,pam->ahjp",
                query_head_rows,
                key_tile_block,
                preferred_element_type=jnp.float32,
            )
            * scaling
        )
        return (jnp.where(seen, scores, NEG_FILL), key_tile_block, value_tile_block, start)

    row_max = jnp.max(local_scores, axis=-1)
    row_sum = jnp.sum(jnp.exp(local_scores - row_max[..., None]), axis=-1)

    def gather_stats(block_index, stats):
        old_max, old_sum = stats
        scores = beacon_scores(block_index)[0]
        new_max = jnp.maximum(old_max, jnp.max(scores, axis=-1))
        updated_sum = old_sum * jnp.exp(old_max - new_max) + jnp.sum(
            jnp.exp(scores - new_max[..., None]), axis=-1
        )
        return (new_max, updated_sum)

    row_max, row_sum = lax.fori_loop(0, block_count, gather_stats, (row_max, row_sum))

    def normalize(scores):
        return jnp.exp(scores - row_max[..., None]) / row_sum[..., None]

    local_probs = normalize(local_scores)
    local_probs_low = local_probs.astype(jnp.bfloat16)
    attended = jnp.einsum(
        "kgwv,vkd->wkgd", local_probs_low, value_heads, preferred_element_type=jnp.float32
    )

    def add_values(block_index, running):
        scores, key_tile_block, value_tile_block, start = beacon_scores(block_index)
        reduced_probability = normalize(scores).astype(jnp.bfloat16)
        return running + jnp.einsum(
            "lupa,alx->plux",
            reduced_probability,
            value_tile_block,
            preferred_element_type=jnp.float32,
        )

    attended = lax.fori_loop(0, block_count, add_values, attended).astype(jnp.bfloat16)
    row_dot = jnp.einsum(
        "wkgd,wkgd->kgw", head_gradients, attended, preferred_element_type=jnp.float32
    )[..., None]
    local_dprob = jnp.einsum(
        "wkgd,vkd->kgwv", head_gradients, value_heads, preferred_element_type=jnp.float32
    )
    local_grad_scores = (local_probs * (local_dprob - row_dot)).astype(jnp.bfloat16)
    query_grad = jnp.einsum(
        "kgwv,vkd->wkgd", local_grad_scores, key_heads, preferred_element_type=jnp.float32
    )
    key_grad = (
        jnp.einsum(
            "kgwv,wkgd->vkd", local_grad_scores, query_head_rows, preferred_element_type=jnp.float32
        )
        * scaling
    )
    value_grad = jnp.einsum(
        "kgwv,wkgd->vkd", local_probs_low, head_gradients, preferred_element_type=jnp.float32
    )

    def add_grads(block_index, carried):
        query_count_total, key_buffer, value_buffer = carried
        scores, key_tile_block, value_tile_block, start = beacon_scores(block_index)
        probabilities = normalize(scores)
        reduced_probability = probabilities.astype(jnp.bfloat16)
        dprob = jnp.einsum(
            "jahm,pam->ahjp", head_gradients, value_tile_block, preferred_element_type=jnp.float32
        )
        score_gradient = (probabilities * (dprob - row_dot)).astype(jnp.bfloat16)
        query_count_total = query_count_total + jnp.einsum(
            "lupa,alx->plux", score_gradient, key_tile_block, preferred_element_type=jnp.float32
        )
        key_part = (
            jnp.einsum(
                "ecxr,xecz->rez",
                score_gradient,
                query_head_rows,
                preferred_element_type=jnp.float32,
            )
            * scaling
        )
        value_part = jnp.einsum(
            "ecxr,xecz->rez",
            reduced_probability,
            head_gradients,
            preferred_element_type=jnp.float32,
        )
        key_buffer = lax.dynamic_update_slice_in_dim(key_buffer, key_part, start, 0)
        value_buffer = lax.dynamic_update_slice_in_dim(value_buffer, value_part, start, 0)
        return (query_count_total, key_buffer, value_buffer)

    empty_buffer = jnp.zeros((beacon_total, kv_local, HD), jnp.float32)
    query_grad, key_buffer, value_buffer = lax.fori_loop(
        0, block_count, add_grads, (query_grad, empty_buffer, empty_buffer)
    )
    query_grad = (query_grad * scaling).astype(jnp.bfloat16)
    own_keys, own_values = (
        lax.psum_scatter(
            key_buffer.astype(jnp.bfloat16), "ctx", scatter_dimension=0, tiled=True
        ).astype(jnp.float32),
        lax.psum_scatter(
            value_buffer.astype(jnp.bfloat16), "ctx", scatter_dimension=0, tiled=True
        ).astype(jnp.float32),
    )
    key_grad = key_grad.at[positions].add(own_keys)
    value_grad = value_grad.at[positions].add(own_values)
    attended_out = attended.reshape(window, group_size * kv_local * HD)
    query_out = query_grad.reshape(window, group_size * kv_local * HD)
    key_out = key_grad.astype(jnp.bfloat16).reshape(window, kv_local * HD)
    value_out = value_grad.astype(jnp.bfloat16).reshape(window, kv_local * HD)
    return (
        lax.all_to_all(attended_out, "head", split_axis=0, concat_axis=1, tiled=True),
        lax.all_to_all(query_out, "head", split_axis=0, concat_axis=1, tiled=True),
        lax.all_to_all(key_out, "head", split_axis=0, concat_axis=1, tiled=True),
        lax.all_to_all(value_out, "head", split_axis=0, concat_axis=1, tiled=True),
    )


def solution(mesh):
    in_specs = (
        P(("ctx", "head"), None),
        P(("ctx", "head"), None),
        P(("ctx", "head"), None),
        P(("ctx", "head"), None),
        P("ctx", None),
    )
    out_specs = (
        P(("ctx", "head"), None),
        P(("ctx", "head"), None),
        P(("ctx", "head"), None),
        P(("ctx", "head"), None),
    )
    return jax.shard_map(local, mesh=mesh, in_specs=in_specs, out_specs=out_specs, check_vma=False)
```

profile of v0, /device:TPU:0, one launch (start us, length us, event | category | flops | bytes accessed | tf_op | source)
XLA Modules:
  0.0 285.3 jit_solution(10834364162672158835)
XLA Ops:
  8.8 6.3 %all-to-all-start = ((bf16[128,4,256]{2,0,1:T(8,128)(2,1)}), bf16[128,4,256]{2,0,1:T(8,128)(2,1)S(1)}, u32[]{:S(2)}, u32[]{:S(2)}) async-start(bf16[128,4,256]{2,0,1:T(8,128)(2,1)} %bitcast.156), calls=%async_computation | async-start | bytes 524288 | tf_op jit(solution)/shard_map/all_to_all | solution.py:13
  16.8 7.2 %all-to-all-done = bf16[128,4,256]{2,0,1:T(8,128)(2,1)S(1)} async-done(((bf16[128,4,256]{2,0,1:T(8,128)(2,1)}), bf16[128,4,256]{2,0,1:T(8,128)(2,1)S(1)}, u32[]{:S(2)}, u32[]{:S(2)}) %all-to-all-start) | async-done | bytes 262176 | tf_op jit(solution)/shard_map/all_to_all | solution.py:13
  29.8 4.7 %all-to-all-done.2 = bf16[128,4,256]{2,0,1:T(8,128)(2,1)S(1)} async-done(((bf16[128,4,256]{2,0,1:T(8,128)(2,1)}), bf16[128,4,256]{2,0,1:T(8,128)(2,1)S(1)}, u32[]{:S(2)}, u32[]{:S(2)}) %all-to-all-start.2) | async-done | bytes 262176 | tf_op jit(solution)/shard_map/all_to_all | solution.py:14
  34.5 3.5 %all-to-all-start.1 = ((bf16[128,4,1024]{2,0,1:T(8,128)(2,1)}), bf16[128,4,1024]{2,0,1:T(8,128)(2,1)S(1)}, u32[]{:S(2)}, u32[]{:S(2)}) async-start(bf16[128,4,1024]{2,0,1:T(8,128)(2,1)} %bitcast.154), calls=%async_computation.1 | async-start | bytes 2097152 | tf_op jit(solution)/shard_map/all_to_all | solution.py:12
  40.3 20.7 %all-to-all-done.1 = bf16[128,4,1024]{2,0,1:T(8,128)(2,1)S(1)} async-done(((bf16[128,4,1024]{2,0,1:T(8,128)(2,1)}), bf16[128,4,1024]{2,0,1:T(8,128)(2,1)S(1)}, u32[]{:S(2)}, u32[]{:S(2)}) %all-to-all-start.1) | async-done | bytes 1048608 | tf_op jit(solution)/shard_map/all_to_all | solution.py:12
  61.0 3.5 %all-to-all-start.4 = ((bf16[128,4,1024]{2,0,1:T(8,128)(2,1)}), bf16[128,4,1024]{2,0,1:T(8,128)(2,1)S(1)}, u32[]{:S(2)}, u32[]{:S(2)}) async-start(bf16[128,4,1024]{2,0,1:T(8,128)(2,1)} %bitcast.153), calls=%async_computation.4 | async-start | bytes 2097152 | tf_op jit(solution)/shard_map/all_to_all | solution.py:15
  66.1 9.3 %all-gather = bf16[512,256]{1,0:T(8,128)(2,1)S(1)} all-gather(bf16[64,256]{1,0:T(8,128)(2,1)S(1)} %gather_fusion), channel_id=2, replica_groups=mesh['ctx'=8,'head'=4] {'ctx'}, dimensions={0}, use_global_device_ids=true | all-gather | bytes 294912 | tf_op jit(solution)/shard_map/all_gather | solution.py:27
  77.0 9.3 %all-gather.1 = bf16[512,256]{1,0:T(8,128)(2,1)S(1)} all-gather(bf16[64,256]{1,0:T(8,128)(2,1)S(1)} %gather_fusion.1), channel_id=3, replica_groups=mesh['ctx'=8,'head'=4] {'ctx'}, dimensions={0}, use_global_device_ids=true | all-gather | bytes 294912 | tf_op jit(solution)/shard_map/all_gather | solution.py:28
  100.2 3.5 %fusion.21 = f32[512,2,128]{2,0,1:T(8,128)} fusion(bf16[512,2,4,128]{3,2,1,0:T(4,128)(2,1)S(1)} %reshape.114, f32[2,512,512,4]{2,1,3,0:T(8,128)S(1)} %get-tuple-element.77, f32[2,4,512]{2,1,0:T(4,128)S(1)} %bitcast.189, f32[2,4,512]{2,1,0:T(4,128)S(1)} %max.11, pred[512,512]{0,1:T(8,128)(4,1)S(1)} %copy-done.6), kind=kOutput, calls=%fused_computation.34 | convolution fusion | flops 547356672 | bytes 10256384 | tf_op jit(solution)/shard_map/kgwv,wkgd->vkd/dot_general | solution.py:111
  105.7 5.3 %fusion.13 = f32[2,128,4,512]{1,3,2,0:T(8,128)S(1)} fusion(bf16[512,2,128,1]{0,2,3,1:T(8,128)(2,1)S(1)} %bitcast.174, f32[2,4,512,512]{2,3,1,0:T(8,128)} %copy-done), kind=kOutput, calls=%fused_computation.28 | convolution fusion | flops 538968064 | bytes 10747904 | tf_op jit(solution)/shard_map/while/body/eval_jaxpr/lupa,alx->plux/dot_general | solution.py:87
  111.4 4.0 %bitcast_convert_fusion = (f32[2,4,512,128]{3,2,1,0:T(8,128)S(1)}, bf16[512,2,4,128]{3,0,2,1:T(8,128)(2,1)}) fusion(f32[2,128,4,512]{1,3,2,0:T(8,128)S(1)} %fusion.13, bf16[512,2,128,1]{2,1,0,3:T(2,128)(2,1)S(1)} %bitcast.184, f32[2,4,512]{2,1,0:T(4,128)S(1)} %bitcast.190, f32[2,4,512]{2,1,0:T(4,128)S(1)} %max.11, f32[2,512,512,4]{2,1,3,0:T(8,128)S(1)} %copy-done.2, ...), kind=kOutput, calls=%fused_computation.47 | convolution fusion | flops 548929536 | bytes 14188544 | tf_op jit(solution)/shard_map/kgwv,vkd->wkgd/dot_general | solution.py:80
  117.7 6.8 %fusion.3 = bf16[2,4,512,512]{2,3,1,0:T(8,128)(2,1)} fusion(f32[2,4,512]{2,1,0:T(4,128)S(1)} %copy.112, bf16[512,2,4,128]{3,2,1,0:T(4,128)(2,1)S(1)} %reshape.114, bf16[512,2,128,1]{2,1,0,3:T(2,128)(2,1)} %bitcast.183, f32[2,4,512]{2,1,0:T(4,128)S(1)} %bitcast.191, f32[2,4,512]{2,1,0:T(4,128)S(1)} %max.11, f32[2,512,512,4]{2,1,3,0:T(8,128)} %copy-done.1, ...), kind=kOutput, calls=%fused_computation.9 | convolution fusion | flops 551550976 | bytes 14204928 | tf_op jit(solution)/shard_map/wkgd,vkd->kgwv/dot_general | solution.py:98
  124.5 6.7 %fusion.1 = bf16[2,4,512,512]{2,3,1,0:T(8,128)(2,1)} fusion(f32[2,4,512,512]{2,3,1,0:T(8,128)} %copy-done, f32[2,4,512]{2,1,0:T(4,128)S(1)} %copy.112, bf16[512,2,128,1]{0,2,3,1:T(8,128)(2,1)S(1)} %bitcast.175, bf16[512,2,4,128]{3,2,1,0:T(4,128)(2,1)S(1)} %reshape.114), kind=kOutput, calls=%fused_computation.6 | convolution fusion | flops 543162368 | bytes 13910016 | tf_op jit(solution)/shard_map/while/body/eval_jaxpr/jahm,pam->ahjp/dot_general | solution.py:120
  131.7 4.1 %fusion.37 = bf16[512,2,128]{2,0,1:T(8,128)(2,1)} fusion(bf16[2,4,512,512]{2,3,1,0:T(8,128)(2,1)} %fusion.1, bf16[512,2,4,128]{3,2,1,0:T(4,128)(2,1)S(1)} %reshape.110), kind=kOutput, calls=%fused_computation.44 | convolution fusion | flops 537133056 | bytes 5505024 | tf_op jit(solution)/shard_map/while/body/eval_jaxpr/ecxr,xecz->rez/dot_general | solution.py:128
  135.9 28.9 %reduce-scatter.5.cloned.1.call-done = bf16[64,2,128]{2,0,1:T(8,128)(2,1)} async-done(((bf16[512,2,128]{2,0,1:T(8,128)(2,1)}), bf16[64,2,128]{2,0,1:T(8,128)(2,1)}) %reduce-scatter.5.cloned.1.call-update) | async-done | bytes 32784 | tf_op jit(solution)/shard_map/reduce_scatter | solution.py:155
  169.4 4.6 %all-to-all-start.7 = ((bf16[4,128,256]{2,1,0:T(8,128)(2,1)}), bf16[4,128,256]{2,1,0:T(8,128)(2,1)}, u32[]{:S(2)}, u32[]{:S(2)}) async-start(bf16[4,128,256]{2,1,0:T(8,128)(2,1)} %all_to_all.134), calls=%async_computation.9 | async-start | bytes 524288 | tf_op jit(solution)/shard_map/all_to_all | solution.py:169
  174.0 3.6 %fusion.28 = f32[512,2,128]{2,0,1:T(8,128)S(1)} fusion(bf16[2,4,512,512]{2,3,1,0:T(8,128)(2,1)} %fusion.3, bf16[512,2,4,128]{3,2,1,0:T(4,128)(2,1)S(1)} %reshape.110), kind=kOutput, calls=%fused_computation.39 | convolution fusion | flops 537001984 | bytes 5767168 | tf_op jit(solution)/shard_map/kgwv,wkgd->vkd/dot_general | solution.py:106
  179.8 22.4 %reduce-scatter.3.cloned.1.call-done = bf16[64,2,128]{2,0,1:T(8,128)(2,1)} async-done(((bf16[512,2,128]{2,0,1:T(8,128)(2,1)}), bf16[64,2,128]{2,0,1:T(8,128)(2,1)}) %reduce-scatter.3.cloned.1.call-update) | async-done | bytes 32784 | tf_op jit(solution)/shard_map/reduce_scatter | solution.py:152
  206.9 4.8 %all-to-all-start.6 = ((bf16[4,128,256]{2,1,0:T(8,128)(2,1)}), bf16[4,128,256]{2,1,0:T(8,128)(2,1)}, u32[]{:S(2)}, u32[]{:S(2)}) async-start(bf16[4,128,256]{2,1,0:T(8,128)(2,1)} %all_to_all.130), calls=%async_computation.7 | async-start | bytes 524288 | tf_op jit(solution)/shard_map/all_to_all | solution.py:168
  211.6 3.9 %fusion.9 = bf16[512,2,4,128]{3,0,2,1:T(8,128)(2,1)S(1)} fusion(f32[2,4,512,128]{3,2,1,0:T(8,128)S(1)} %fusion.50, bf16[512,2,128,1]{0,2,3,1:T(8,128)(2,1)S(1)} %bitcast.173, bf16[2,4,512,512]{2,3,1,0:T(8,128)(2,1)} %fusion.1), kind=kOutput, calls=%fused_computation.22 | convolution fusion | flops 538443776 | bytes 7602176 | tf_op jit(solution)/shard_map/while/body/eval_jaxpr/lupa,alx->plux/dot_general | solution.py:124
  220.1 3.8 %all-to-all-start.5 = ((bf16[4,128,1024]{2,1,0:T(8,128)(2,1)}), bf16[4,128,1024]{2,1,0:T(8,128)(2,1)S(1)}, u32[]{:S(2)}, u32[]{:S(2)}) async-start(bf16[4,128,1024]{2,1,0:T(8,128)(2,1)} %all_to_all.126), calls=%async_computation.5 | async-start | bytes 2097152 | tf_op jit(solution)/shard_map/all_to_all | solution.py:167
  226.3 21.5 %all-to-all-done.5 = bf16[4,128,1024]{2,1,0:T(8,128)(2,1)S(1)} async-done(((bf16[4,128,1024]{2,1,0:T(8,128)(2,1)}), bf16[4,128,1024]{2,1,0:T(8,128)(2,1)S(1)}, u32[]{:S(2)}, u32[]{:S(2)}) %all-to-all-start.5) | async-done | bytes 1048608 | tf_op jit(solution)/shard_map/all_to_all | solution.py:167
  247.8 3.5 %all-to-all-start.3 = ((bf16[4,128,1024]{2,1,0:T(8,128)(2,1)}), bf16[4,128,1024]{2,1,0:T(8,128)(2,1)S(1)}, u32[]{:S(2)}, u32[]{:S(2)}) async-start(bf16[4,128,1024]{2,1,0:T(8,128)(2,1)} %all_to_all.119), calls=%async_computation.3 | async-start | bytes 2097152 | tf_op jit(solution)/shard_map/all_to_all | solution.py:166
  256.7 19.9 %all-to-all-done.3 = bf16[4,128,1024]{2,1,0:T(8,128)(2,1)S(1)} async-done(((bf16[4,128,1024]{2,1,0:T(8,128)(2,1)}), bf16[4,128,1024]{2,1,0:T(8,128)(2,1)S(1)}, u32[]{:S(2)}, u32[]{:S(2)}) %all-to-all-start.3) | async-done | bytes 1048608 | tf_op jit(solution)/shard_map/all_to_all | solution.py:166
  (77 shorter events, 59.0 us)
Async XLA Ops:
  7.2 57.4 %copy-start.10 = (s32[1,64]{1,0:T(1,128)S(1)}, s32[1,64]{1,0:T(1,128)}, u32[]{:S(2)}) copy-start(s32[1,64]{1,0:T(1,128)} %param.9) | copy-start | bytes 772
  8.8 15.2 %all-to-all-start = ((bf16[128,4,256]{2,0,1:T(8,128)(2,1)}), bf16[128,4,256]{2,0,1:T(8,128)(2,1)S(1)}, u32[]{:S(2)}, u32[]{:S(2)}) async-start(bf16[128,4,256]{2,0,1:T(8,128)(2,1)} %bitcast.156), calls=%async_computation | async-start | bytes 524288 | tf_op jit(solution)/shard_map/all_to_all | solution.py:13
  24.1 10.4 %all-to-all-start.2 = ((bf16[128,4,256]{2,0,1:T(8,128)(2,1)}), bf16[128,4,256]{2,0,1:T(8,128)(2,1)S(1)}, u32[]{:S(2)}, u32[]{:S(2)}) async-start(bf16[128,4,256]{2,0,1:T(8,128)(2,1)} %bitcast.155), calls=%async_computation.2 | async-start | bytes 524288 | tf_op jit(solution)/shard_map/all_to_all | solution.py:14
  34.5 26.5 %all-to-all-start.1 = ((bf16[128,4,1024]{2,0,1:T(8,128)(2,1)}), bf16[128,4,1024]{2,0,1:T(8,128)(2,1)S(1)}, u32[]{:S(2)}, u32[]{:S(2)}) async-start(bf16[128,4,1024]{2,0,1:T(8,128)(2,1)} %bitcast.154), calls=%async_computation.1 | async-start | bytes 2097152 | tf_op jit(solution)/shard_map/all_to_all | solution.py:12
  61.0 28.4 %all-to-all-start.4 = ((bf16[128,4,1024]{2,0,1:T(8,128)(2,1)}), bf16[128,4,1024]{2,0,1:T(8,128)(2,1)S(1)}, u32[]{:S(2)}, u32[]{:S(2)}) async-start(bf16[128,4,1024]{2,0,1:T(8,128)(2,1)} %bitcast.153), calls=%async_computation.4 | async-start | bytes 2097152 | tf_op jit(solution)/shard_map/all_to_all | solution.py:15
  64.5 100.3 %reduce-scatter.5.cloned.1.call-start = ((), (), s32[]{:S(2)}) async-start(), calls=%async_computation.11 | async-start | bytes 294912 | tf_op jit(solution)/shard_map/reduce_scatter | solution.py:155
  90.1 2.2 copy-start.5
  90.1 2.2 copy-start.6
  94.0 6.1 %copy-start.1 = (f32[2,512,512,4]{2,1,3,0:T(8,128)}, f32[2,512,512,4]{2,1,3,0:T(8,128)S(1)}, u32[]{:S(2)}) copy-start(f32[2,512,512,4]{2,1,3,0:T(8,128)S(1)} %get-tuple-element.77) | copy-start | bytes 25165828
  100.1 3.6 %copy-start = (f32[2,4,512,512]{2,3,1,0:T(8,128)}, f32[2,4,512,512]{2,3,1,0:T(8,128)S(1)}, u32[]{:S(2)}) copy-start(f32[2,4,512,512]{2,3,1,0:T(8,128)S(1)} %fusion.6) | copy-start | bytes 25165828
  103.7 2.0 copy-start.4
  103.7 7.3 %copy-start.9 = (bf16[512,2,128]{2,1,0:T(2,128)(2,1)S(1)}, bf16[512,2,128]{2,1,0:T(2,128)(2,1)}, u32[]{:S(2)}) copy-start(bf16[512,2,128]{2,1,0:T(2,128)(2,1)} %reshape.112) | copy-start | bytes 786436
  105.7 5.8 %copy-start.2 = (f32[2,512,512,4]{2,1,3,0:T(8,128)S(1)}, f32[2,512,512,4]{2,1,3,0:T(8,128)}, u32[]{:S(2)}) copy-start(f32[2,512,512,4]{2,1,3,0:T(8,128)} %copy-done.1) | copy-start | bytes 25165828
  124.5 6.8 %copy-start.8 = (f32[512,2,128]{2,0,1:T(8,128)S(1)}, f32[512,2,128]{2,0,1:T(8,128)}, u32[]{:S(2)}) copy-start(f32[512,2,128]{2,0,1:T(8,128)} %fusion.21) | copy-start | bytes 1572868
  131.2 71.0 %reduce-scatter.3.cloned.1.call-start = ((), (), s32[]{:S(2)}) async-start(), calls=%async_computation.10 | async-start | bytes 294912 | tf_op jit(solution)/shard_map/reduce_scatter | solution.py:152
  169.4 37.5 %all-to-all-start.7 = ((bf16[4,128,256]{2,1,0:T(8,128)(2,1)}), bf16[4,128,256]{2,1,0:T(8,128)(2,1)}, u32[]{:S(2)}, u32[]{:S(2)}) async-start(bf16[4,128,256]{2,1,0:T(8,128)(2,1)} %all_to_all.134), calls=%async_computation.9 | async-start | bytes 524288 | tf_op jit(solution)/shard_map/all_to_all | solution.py:169
  174.0 4.0 %copy-start.3 = (bf16[2,4,512,512]{2,3,1,0:T(8,128)(2,1)S(1)}, bf16[2,4,512,512]{2,3,1,0:T(8,128)(2,1)}, u32[]{:S(2)}) copy-start(bf16[2,4,512,512]{2,3,1,0:T(8,128)(2,1)} %fusion.3) | copy-start | bytes 12582916
  206.9 17.0 %copy-start.7 = (bf16[512,2,4,128]{3,0,2,1:T(8,128)(2,1)S(1)}, bf16[512,2,4,128]{3,0,2,1:T(8,128)(2,1)}, u32[]{:S(2)}) copy-start(bf16[512,2,4,128]{3,0,2,1:T(8,128)(2,1)} %get-tuple-element.81) | copy-start | bytes 3145732
  206.9 13.2 %all-to-all-start.6 = ((bf16[4,128,256]{2,1,0:T(8,128)(2,1)}), bf16[4,128,256]{2,1,0:T(8,128)(2,1)}, u32[]{:S(2)}, u32[]{:S(2)}) async-start(bf16[4,128,256]{2,1,0:T(8,128)(2,1)} %all_to_all.130), calls=%async_computation.7 | async-start | bytes 524288 | tf_op jit(solution)/shard_map/all_to_all | solution.py:168
  220.1 27.7 %all-to-all-start.5 = ((bf16[4,128,1024]{2,1,0:T(8,128)(2,1)}), bf16[4,128,1024]{2,1,0:T(8,128)(2,1)S(1)}, u32[]{:S(2)}, u32[]{:S(2)}) async-start(bf16[4,128,1024]{2,1,0:T(8,128)(2,1)} %all_to_all.126), calls=%async_computation.5 | async-start | bytes 2097152 | tf_op jit(solution)/shard_map/all_to_all | solution.py:167
  247.8 28.7 %all-to-all-start.3 = ((bf16[4,128,1024]{2,1,0:T(8,128)(2,1)}), bf16[4,128,1024]{2,1,0:T(8,128)(2,1)S(1)}, u32[]{:S(2)}, u32[]{:S(2)}) async-start(bf16[4,128,1024]{2,1,0:T(8,128)(2,1)} %all_to_all.119), calls=%async_computation.3 | async-start | bytes 2097152 | tf_op jit(solution)/shard_map/all_to_all | solution.py:166
Sparse Core Ops, SparseCore 0:
  131.3 33.3 reduce-scatter.4
  168.7 33.5 reduce-scatter.2
where the time goes:
time: 286 us; the launch traced here: 285 us
  waiting for transfers between devices  128 us (45%)
  matrix products  45.5 us (16%)
  starting transfers between devices  33.5 us (12%)
  local copies, waits for them, and re-layouts  30.2 us (11%)
  blocking collectives  18.6 us (7%)
  other arithmetic  14.8 us (5%)
  between operations  14.4 us (5%)
    reduce_scatter x1, waiting for transfers between devices, local(): lax.psum_scatter(value_buffer.astype(jnp.bfloat16), 'ctx', scatter_dimens...  28.9 us
    reduce_scatter x1, waiting for transfers between devices, local(): lax.psum_scatter(key_buffer.astype(jnp.bfloat16), 'ctx', scatter_dimensio...  22.4 us
    all_to_all x1, waiting for transfers between devices, local(): lax.all_to_all(query_out, 'head', split_axis=0, concat_axis=1, tiled=True)  21.5 us
    all_to_all x1, waiting for transfers between devices, local(): lax.all_to_all(queries, 'head', split_axis=1, concat_axis=0, tiled=True)  20.7 us
    all_to_all x1, waiting for transfers between devices, local(): lax.all_to_all(attended_out, 'head', split_axis=0, concat_axis=1, tiled=T...  19.9 us
    all_gather x1, blocking collectives, local(): lax.all_gather(key_rows[positions], 'ctx', axis=0, tiled=True)  9.32 us
    all_gather x1, blocking collectives, local(): lax.all_gather(value_rows[positions], 'ctx', axis=0, tiled=True)  9.29 us
    all_to_all x1, waiting for transfers between devices, local(): lax.all_to_all(keys, 'head', split_axis=1, concat_axis=0, tiled=True)  7.25 us
  transfers between devices with their start and end apart: 10, of which 9 were waited for; matrix products, arithmetic and copies ran while one was open for 14% of the time, Pallas kernels for 0%

commit v1 on v0

--- a/solution.py
+++ b/solution.py
@@ -163,7 +163,12 @@
     key_out = key_grad.astype(jnp.bfloat16).reshape(window, kv_local * HD)
     value_out = value_grad.astype(jnp.bfloat16).reshape(window, kv_local * HD)
     return (
-        lax.all_to_all(attended_out, "head", split_axis=0, concat_axis=1, tiled=True),
+        jnp.concatenate(
+            lax.all_to_all(
+                jnp.stack(jnp.split(attended_out, lax.axis_size("head"), axis=0)), "head", 0, 0
+            ),
+            axis=1,
+        ),
         lax.all_to_all(query_out, "head", split_axis=0, concat_axis=1, tiled=True),
         lax.all_to_all(key_out, "head", split_axis=0, concat_axis=1, tiled=True),
         lax.all_to_all(value_out, "head", split_axis=0, concat_axis=1, tiled=True),

time: 286 us -> 265 us (0.927)
  waiting for transfers between devices: 128 us -> 92 us
  other arithmetic: 14.8 us -> 21.4 us
  local copies, waits for them, and re-layouts: 30.2 us -> 35.7 us
    reduce_scatter x1, waiting for transfers between devices: 28.9 us -> 0.02 us  [local(): lax.psum_scatter(value_buffer.astype(jnp.bfloat16), 'ctx', scatter_dimens...]
    all_to_all x1, waiting for transfers between devices: 20.7 us -> 0.01 us  [local(): lax.all_to_all(queries, 'head', split_axis=1, concat_axis=0, tiled=True)]
    all_to_all x1, waiting for transfers between devices: 0.65 us -> 13.5 us  [local(): lax.all_to_all(out_grad, 'head', split_axis=1, concat_axis=0, tiled=True)]
    unnamed x24 -> x39, local copies, waits for them, and re-layouts: 3.13 us -> 8.68 us
    dot_general x1, matrix products: 3.96 us -> 7.83 us  [local(): jnp.einsum('kgwv,vkd->wkgd', local_probs_low, value_heads, preferred_elem...]
    dot_general x1, matrix products: 2.19 us -> 5.24 us  [beacon_scores(): jnp.einsum('jahm,pam->ahjp', query_head_rows, key_tile_block, preferred_e...]
  transfers between devices with their start and end apart: 10 -> 10, of which waited for: 9 -> 7; matrix products, arithmetic and copies ran while one was open for 14% -> 30% of each run, Pallas kernels for 0% -> 0%
where the time goes in v1:
time: 265 us; the launch traced here: 264 us
  waiting for transfers between devices  92 us (35%)
  matrix products  47.4 us (18%)
  local copies, waits for them, and re-layouts  35.7 us (13%)
  starting transfers between devices  34.2 us (13%)
  other arithmetic  21.4 us (8%)
  blocking collectives  18.6 us (7%)
  between operations  14.5 us (5%)
    all_to_all x1, waiting for transfers between devices, local(): lax.all_to_all(query_out, 'head', split_axis=0, concat_axis=1, tiled=True)  22.8 us
    reduce_scatter x1, waiting for transfers between devices, local(): lax.psum_scatter(key_buffer.astype(jnp.bfloat16), 'ctx', scatter_dimensio...  21.7 us
    all_to_all x1, waiting for transfers between devices, local(): lax.all_to_all(jnp.stack(jnp.split(attended_out, lax.axis_size('head'), a...  19.9 us
    all_to_all x1, waiting for transfers between devices, local(): lax.all_to_all(out_grad, 'head', split_axis=1, concat_axis=0, tiled=True)  13.5 us
    all_gather x1, blocking collectives, local(): lax.all_gather(key_rows[positions], 'ctx', axis=0, tiled=True)  9.32 us
    all_gather x1, blocking collectives, local(): lax.all_gather(value_rows[positions], 'ctx', axis=0, tiled=True)  9.29 us
    unnamed x39, local copies, waits for them, and re-layouts  8.68 us
    dot_general x1, matrix products, local(): jnp.einsum('wkgd,vkd->kgwv', head_gradients, value_heads, preferred_eleme...  8.24 us
  transfers between devices with their start and end apart: 10, of which 7 were waited for; matrix products, arithmetic and copies ran while one was open for 30% of the time, Pallas kernels for 0%

profile of v1, /device:TPU:0, one launch (start us, length us, event | category | flops | bytes accessed | tf_op | source)
XLA Modules:
  0.0 263.8 jit_solution(3502824906890383495)
XLA Ops:
  8.8 6.3 %all-to-all-start = ((bf16[128,4,256]{2,0,1:T(8,128)(2,1)}), bf16[128,4,256]{2,0,1:T(8,128)(2,1)S(1)}, u32[]{:S(2)}, u32[]{:S(2)}) async-start(bf16[128,4,256]{2,0,1:T(8,128)(2,1)} %bitcast.169), calls=%async_computation | async-start | bytes 524288 | tf_op jit(solution)/shard_map/all_to_all | solution.py:13
  17.0 7.1 %all-to-all-done = bf16[128,4,256]{2,0,1:T(8,128)(2,1)S(1)} async-done(((bf16[128,4,256]{2,0,1:T(8,128)(2,1)}), bf16[128,4,256]{2,0,1:T(8,128)(2,1)S(1)}, u32[]{:S(2)}, u32[]{:S(2)}) %all-to-all-start) | async-done | bytes 262176 | tf_op jit(solution)/shard_map/all_to_all | solution.py:13
  29.8 4.7 %all-to-all-done.2 = bf16[128,4,256]{0,2,1:T(8,128)(2,1)S(1)} async-done(((bf16[128,4,256]{0,2,1:T(8,128)(2,1)}), bf16[128,4,256]{0,2,1:T(8,128)(2,1)S(1)}, u32[]{:S(2)}, u32[]{:S(2)}) %all-to-all-start.2) | async-done | bytes 262176 | tf_op jit(solution)/shard_map/all_to_all | solution.py:14
  34.5 3.5 %all-to-all-start.1 = ((bf16[128,4,1024]{2,0,1:T(8,128)(2,1)}), bf16[128,4,1024]{2,0,1:T(8,128)(2,1)S(1)}, u32[]{:S(2)}, u32[]{:S(2)}) async-start(bf16[128,4,1024]{2,0,1:T(8,128)(2,1)} %bitcast.168), calls=%async_computation.1 | async-start | bytes 2097152 | tf_op jit(solution)/shard_map/all_to_all | solution.py:12
  44.5 9.3 %all-gather = bf16[512,256]{1,0:T(8,128)(2,1)S(1)} all-gather(bf16[64,256]{1,0:T(8,128)(2,1)S(1)} %gather_fusion), channel_id=2, replica_groups=mesh['ctx'=8,'head'=4] {'ctx'}, dimensions={0}, use_global_device_ids=true | all-gather | bytes 294912 | tf_op jit(solution)/shard_map/all_gather | solution.py:27
  54.7 9.3 %all-gather.1 = bf16[512,256]{1,0:T(8,128)(2,1)S(1)} all-gather(bf16[64,256]{1,0:T(8,128)(2,1)S(1)} %gather_fusion.1), channel_id=3, replica_groups=mesh['ctx'=8,'head'=4] {'ctx'}, dimensions={0}, use_global_device_ids=true | all-gather | bytes 294912 | tf_op jit(solution)/shard_map/all_gather | solution.py:28
  64.9 5.1 %all-to-all-start.4 = ((bf16[128,4,1024]{2,0,1:T(8,128)(2,1)}), bf16[128,4,1024]{2,0,1:T(8,128)(2,1)S(1)}, u32[]{:S(2)}, u32[]{:S(2)}) async-start(bf16[128,4,1024]{2,0,1:T(8,128)(2,1)} %bitcast.167), calls=%async_computation.4 | async-start | bytes 2097152 | tf_op jit(solution)/shard_map/all_to_all | solution.py:15
  70.7 5.2 %bitcast_reduce_fusion = (f32[2,4,512]{2,1,0:T(4,128)S(1)}, f32[2,512,512,4]{2,1,3,0:T(8,128)}) fusion(pred[512]{0:T(512)(128)(4,1)S(1)} %fusion.53, bf16[512,2,128,1]{0,2,3,1:T(8,128)(2,1)S(1)} %bitcast.186, bf16[512,2,4,128]{3,2,1,0:T(4,128)(2,1)S(1)} %reshape.120), kind=kOutput, calls=%fused_computation.11 | convolution fusion | flops 543158272 | bytes 9716224 | tf_op jit(solution)/shard_map/while/body/eval_jaxpr/jahm,pam->ahjp/dot_general | solution.py:51
  82.6 13.5 %all-to-all-done.4 = bf16[128,4,1024]{2,0,1:T(8,128)(2,1)S(1)} async-done(((bf16[128,4,1024]{2,0,1:T(8,128)(2,1)}), bf16[128,4,1024]{2,0,1:T(8,128)(2,1)S(1)}, u32[]{:S(2)}, u32[]{:S(2)}) %all-to-all-start.4) | async-done | bytes 1048608 | tf_op jit(solution)/shard_map/all_to_all | solution.py:15
  96.9 4.6 %fusion.7 = f32[2,4,512]{2,1,0:T(4,128)S(1)} fusion(f32[2,512,512,4]{2,1,3,0:T(8,128)} %get-tuple-element.101, f32[2,4,512]{2,1,0:T(4,128)S(1)} %max.11, pred[512]{0:T(512)(128)(4,1)S(1)} %fusion.53), kind=kLoop, calls=%fused_computation.19 | loop fusion | flops 8384512 | bytes 8421888 | tf_op jit(solution)/shard_map/while/body/eval_jaxpr/reduce_sum | solution.py:68
  101.5 4.8 %fusion.6 = f32[2,4,512,512]{2,3,1,0:T(8,128)S(1)} fusion(f32[2,512,512,4]{2,1,3,0:T(8,128)} %get-tuple-element.101, f32[2,4,512]{2,1,0:T(4,128)S(1)} %bitcast.204, f32[2,4,512]{2,1,0:T(4,128)S(1)} %max.11, pred[512]{0:T(512)(128)(4,1)S(1)} %fusion.53), kind=kLoop, calls=%fused_computation.18 | loop fusion | flops 8388608 | bytes 16810496 | tf_op jit(solution)/shard_map/while/body/eval_jaxpr/div | solution.py:76
  112.0 4.1 %fusion.13 = f32[2,128,4,512]{3,1,2,0:T(8,128)S(1)} fusion(bf16[512,2,128,1]{0,2,3,1:T(8,128)(2,1)S(1)} %bitcast.189, f32[2,4,512,512]{2,3,1,0:T(8,128)} %copy-done), kind=kOutput, calls=%fused_computation.28 | convolution fusion | flops 538968064 | bytes 10747904 | tf_op jit(solution)/shard_map/while/body/eval_jaxpr/lupa,alx->plux/dot_general | solution.py:87
  116.1 7.8 %bitcast_convert_fusion = (f32[2,4,512,128]{2,3,1,0:T(8,128)}, bf16[512,2,4,128]{0,3,2,1:T(8,128)(2,1)}) fusion(f32[2,128,4,512]{3,1,2,0:T(8,128)S(1)} %fusion.13, f32[2,4,512]{2,1,0:T(4,128)S(1)} %bitcast.206, f32[2,4,512]{2,1,0:T(4,128)S(1)} %max.11, f32[2,512,512,4]{2,1,3,0:T(8,128)} %copy-done.2, pred[512,512]{0,1:T(8,128)(4,1)S(1)} %copy-done.10, ...), kind=kOutput, calls=%fused_computation.48 | convolution fusion | flops 548929536 | bytes 14188544 | tf_op jit(solution)/shard_map/kgwv,vkd->wkgd/dot_general | solution.py:80
  130.0 4.8 %fusion.1 = bf16[2,4,512,512]{2,3,1,0:T(8,128)(2,1)S(1)} fusion(f32[2,4,512,512]{2,3,1,0:T(8,128)} %copy-done, f32[2,4,512]{2,1,0:T(4,128)S(1)} %copy.145, bf16[512,2,128,1]{0,2,3,1:T(8,128)(2,1)} %bitcast.188, bf16[512,2,4,128]{3,2,1,0:T(4,128)(2,1)S(1)} %reshape.126), kind=kOutput, calls=%fused_computation.6 | convolution fusion | flops 543162368 | bytes 13910016 | tf_op jit(solution)/shard_map/while/body/eval_jaxpr/jahm,pam->ahjp/dot_general | solution.py:120
  134.9 8.2 %fusion.3 = bf16[2,4,512,512]{2,3,1,0:T(8,128)(2,1)} fusion(f32[2,4,512]{2,1,0:T(4,128)S(1)} %copy.145, bf16[512,2,4,128]{3,2,1,0:T(4,128)(2,1)S(1)} %reshape.126, bf16[512,2,128]{0,2,1:T(8,128)(2,1)S(1)} %copy-done.13, f32[2,4,512]{2,1,0:T(4,128)S(1)} %bitcast.207, f32[2,4,512]{2,1,0:T(4,128)S(1)} %max.11, f32[2,512,512,4]{2,1,3,0:T(8,128)} %copy-done.2, ...), kind=kOutput, calls=%fused_computation.9 | convolution fusion | flops 551550976 | bytes 14204928 | tf_op jit(solution)/shard_map/wkgd,vkd->kgwv/dot_general | solution.py:98
  149.7 4.1 %all-to-all-start.7 = ((bf16[4,128,256]{2,1,0:T(8,128)(2,1)}), bf16[4,128,256]{2,1,0:T(8,128)(2,1)}, u32[]{:S(2)}, u32[]{:S(2)}) async-start(bf16[4,128,256]{2,1,0:T(8,128)(2,1)} %all_to_all.120), calls=%async_computation.9 | async-start | bytes 524288 | tf_op jit(solution)/shard_map/all_to_all | solution.py:174
  153.8 3.6 %fusion.28 = f32[512,2,128]{2,0,1:T(8,128)S(1)} fusion(bf16[2,4,512,512]{2,3,1,0:T(8,128)(2,1)} %fusion.3, bf16[512,2,4,128]{3,2,1,0:T(4,128)(2,1)S(1)} %copy-done.4), kind=kOutput, calls=%fused_computation.39 | convolution fusion | flops 537001984 | bytes 5767168 | tf_op jit(solution)/shard_map/kgwv,wkgd->vkd/dot_general | solution.py:106
  159.7 21.7 %reduce-scatter.3.cloned.1.call-done = bf16[64,2,128]{2,0,1:T(8,128)(2,1)} async-done(((bf16[512,2,128]{2,0,1:T(8,128)(2,1)}), bf16[64,2,128]{2,0,1:T(8,128)(2,1)}) %reduce-scatter.3.cloned.1.call-update) | async-done | bytes 32784 | tf_op jit(solution)/shard_map/reduce_scatter | solution.py:152
  186.0 4.7 %all-to-all-start.6 = ((bf16[4,128,256]{2,1,0:T(8,128)(2,1)}), bf16[4,128,256]{2,1,0:T(8,128)(2,1)}, u32[]{:S(2)}, u32[]{:S(2)}) async-start(bf16[4,128,256]{2,1,0:T(8,128)(2,1)} %all_to_all.116), calls=%async_computation.7 | async-start | bytes 524288 | tf_op jit(solution)/shard_map/all_to_all | solution.py:173
  190.7 3.9 %fusion.9 = bf16[512,2,4,128]{3,0,2,1:T(8,128)(2,1)S(1)} fusion(f32[2,4,512,128]{3,2,1,0:T(8,128)S(1)} %fusion.50, bf16[512,2,128,1]{0,2,3,1:T(8,128)(2,1)S(1)} %bitcast.187, bf16[2,4,512,512]{2,3,1,0:T(8,128)(2,1)} %copy-done.1), kind=kOutput, calls=%fused_computation.22 | convolution fusion | flops 538443776 | bytes 7602176 | tf_op jit(solution)/shard_map/while/body/eval_jaxpr/lupa,alx->plux/dot_general | solution.py:124
  199.2 3.5 %all-to-all-start.5 = ((bf16[4,128,1024]{2,1,0:T(8,128)(2,1)}), bf16[4,128,1024]{2,1,0:T(8,128)(2,1)S(1)}, u32[]{:S(2)}, u32[]{:S(2)}) async-start(bf16[4,128,1024]{2,1,0:T(8,128)(2,1)} %all_to_all.112), calls=%async_computation.5 | async-start | bytes 2097152 | tf_op jit(solution)/shard_map/all_to_all | solution.py:172
  204.2 22.8 %all-to-all-done.5 = bf16[4,128,1024]{2,1,0:T(8,128)(2,1)S(1)} async-done(((bf16[4,128,1024]{2,1,0:T(8,128)(2,1)}), bf16[4,128,1024]{2,1,0:T(8,128)(2,1)S(1)}, u32[]{:S(2)}, u32[]{:S(2)}) %all-to-all-start.5) | async-done | bytes 1048608 | tf_op jit(solution)/shard_map/all_to_all | solution.py:172
  226.9 3.5 %all-to-all-start.3 = ((bf16[4,128,1024]{1,2,0:T(8,128)(2,1)}), bf16[4,128,1024]{1,2,0:T(8,128)(2,1)S(1)}, u32[]{:S(2)}, u32[]{:S(2)}) async-start(bf16[4,128,1024]{1,2,0:T(8,128)(2,1)} %pad_maximum_fusion), calls=%async_computation.3 | async-start | bytes 2097152 | tf_op jit(solution)/shard_map/all_to_all | solution.py:167
  235.8 19.9 %all-to-all-done.3 = bf16[4,128,1024]{1,2,0:T(8,128)(2,1)S(1)} async-done(((bf16[4,128,1024]{1,2,0:T(8,128)(2,1)}), bf16[4,128,1024]{1,2,0:T(8,128)(2,1)S(1)}, u32[]{:S(2)}, u32[]{:S(2)}) %all-to-all-start.3) | async-done | bytes 1048608 | tf_op jit(solution)/shard_map/all_to_all | solution.py:167
  (95 shorter events, 63.1 us)
Async XLA Ops:
  7.2 33.2 %copy-start.15 = (s32[1,64]{1,0:T(1,128)S(1)}, s32[1,64]{1,0:T(1,128)}, u32[]{:S(2)}) copy-start(s32[1,64]{1,0:T(1,128)} %param.9) | copy-start | bytes 772
  8.8 15.2 %all-to-all-start = ((bf16[128,4,256]{2,0,1:T(8,128)(2,1)}), bf16[128,4,256]{2,0,1:T(8,128)(2,1)S(1)}, u32[]{:S(2)}, u32[]{:S(2)}) async-start(bf16[128,4,256]{2,0,1:T(8,128)(2,1)} %bitcast.169), calls=%async_computation | async-start | bytes 524288 | tf_op jit(solution)/shard_map/all_to_all | solution.py:13
  24.1 10.4 %all-to-all-start.2 = ((bf16[128,4,256]{0,2,1:T(8,128)(2,1)}), bf16[128,4,256]{0,2,1:T(8,128)(2,1)S(1)}, u32[]{:S(2)}, u32[]{:S(2)}) async-start(bf16[128,4,256]{0,2,1:T(8,128)(2,1)} %bitcast.12), calls=%async_computation.2 | async-start | bytes 524288 | tf_op jit(solution)/shard_map/all_to_all | solution.py:14
  34.5 30.4 %all-to-all-start.1 = ((bf16[128,4,1024]{2,0,1:T(8,128)(2,1)}), bf16[128,4,1024]{2,0,1:T(8,128)(2,1)S(1)}, u32[]{:S(2)}, u32[]{:S(2)}) async-start(bf16[128,4,1024]{2,0,1:T(8,128)(2,1)} %bitcast.168), calls=%async_computation.1 | async-start | bytes 2097152 | tf_op jit(solution)/shard_map/all_to_all | solution.py:12
  64.9 31.3 %all-to-all-start.4 = ((bf16[128,4,1024]{2,0,1:T(8,128)(2,1)}), bf16[128,4,1024]{2,0,1:T(8,128)(2,1)S(1)}, u32[]{:S(2)}, u32[]{:S(2)}) async-start(bf16[128,4,1024]{2,0,1:T(8,128)(2,1)} %bitcast.167), calls=%async_computation.4 | async-start | bytes 2097152 | tf_op jit(solution)/shard_map/all_to_all | solution.py:15
  69.9 75.2 %reduce-scatter.5.cloned.1.call-start = ((), (), s32[]{:S(2)}) async-start(), calls=%async_computation.11 | async-start | bytes 294912 | tf_op jit(solution)/shard_map/reduce_scatter | solution.py:155
  70.7 7.0 %copy-start.3 = (bf16[512,2,4,128]{3,2,1,0:T(4,128)(2,1)}, bf16[512,2,4,128]{3,2,1,0:T(4,128)(2,1)S(1)}, u32[]{:S(2)}) copy-start(bf16[512,2,4,128]{3,2,1,0:T(4,128)(2,1)S(1)} %reshape.120) | copy-start | bytes 3145732
  70.7 5.3 %copy-start.8 = (bf16[512,2,128]{2,1,0:T(2,128)(2,1)S(1)}, bf16[512,2,128]{2,1,0:T(2,128)(2,1)}, u32[]{:S(2)}) copy-start(bf16[512,2,128]{2,1,0:T(2,128)(2,1)} %reshape.119) | copy-start | bytes 786436
  70.7 5.3 %copy-start.10 = (pred[512,512]{0,1:T(8,128)(4,1)S(1)}, pred[512,512]{0,1:T(8,128)(4,1)}, u32[]{:S(2)}) copy-start(pred[512,512]{0,1:T(8,128)(4,1)} %iota_compare_fusion) | copy-start | bytes 786436
  96.9 9.5 %slice-start = ((s8[8388608]{0:T(1024)(128)(4,1)}), s8[4194304]{0:T(1024)(128)(4,1)S(1)}, s32[]{:S(2)}) async-start(s8[8388608]{0:T(1024)(128)(4,1)} %bitcast.175), calls=%async_computation.12 | async-start | bytes 8388608
  101.5 4.9 %slice-start.1 = ((s8[8388608]{0:T(1024)(128)(4,1)}), s8[4194304]{0:T(1024)(128)(4,1)S(1)}, s32[]{:S(2)}) async-start(s8[8388608]{0:T(1024)(128)(4,1)} %bitcast.175), calls=%async_computation.13 | async-start | bytes 8388608
  109.9 6.2 %copy-start.14 = (bf16[512,2,128,1]{0,2,1,3:T(8,128)(2,1)S(1)}, bf16[512,2,128,1]{0,2,1,3:T(8,128)(2,1)}, u32[]{:S(2)}) copy-start(bf16[512,2,128,1]{0,2,1,3:T(8,128)(2,1)} %reshape.163) | copy-start | bytes 786436
  111.9 69.4 %reduce-scatter.3.cloned.1.call-start = ((), (), s32[]{:S(2)}) async-start(), calls=%async_computation.10 | async-start | bytes 294912 | tf_op jit(solution)/shard_map/reduce_scatter | solution.py:152
  128.7 6.1 %copy-start.11 = (pred[512,512]{0,1:T(8,128)(4,1)S(1)}, pred[512,512]{0,1:T(8,128)(4,1)}, u32[]{:S(2)}) copy-start(pred[512,512]{0,1:T(8,128)(4,1)} %iota_compare_fusion) | copy-start | bytes 786436
  128.7 6.1 %copy-start.13 = (bf16[512,2,128]{0,2,1:T(8,128)(2,1)S(1)}, bf16[512,2,128]{0,2,1:T(8,128)(2,1)}, u32[]{:S(2)}) copy-start(bf16[512,2,128]{0,2,1:T(8,128)(2,1)} %reshape.122) | copy-start | bytes 786436
  134.8 8.3 %copy-start.1 = (bf16[2,4,512,512]{2,3,1,0:T(8,128)(2,1)}, bf16[2,4,512,512]{2,3,1,0:T(8,128)(2,1)S(1)}, u32[]{:S(2)}) copy-start(bf16[2,4,512,512]{2,3,1,0:T(8,128)(2,1)S(1)} %fusion.1) | copy-start | bytes 12582916
  134.8 8.3 %copy-start.4 = (bf16[512,2,4,128]{3,2,1,0:T(4,128)(2,1)S(1)}, bf16[512,2,4,128]{3,2,1,0:T(4,128)(2,1)}, u32[]{:S(2)}) copy-start(bf16[512,2,4,128]{3,2,1,0:T(4,128)(2,1)} %copy-done.3) | copy-start | bytes 3145732
  134.9 11.1 %copy-start.6 = (f32[512,2,128]{2,1,0:T(2,128)S(1)}, f32[512,2,128]{2,1,0:T(2,128)}, u32[]{:S(2)}) copy-start(f32[512,2,128]{2,1,0:T(2,128)} %copy.128) | copy-start | bytes 1572868
  143.1 14.7 %copy-start.9 = (bf16[512,2,128]{2,1,0:T(2,128)(2,1)S(1)}, bf16[512,2,128]{2,1,0:T(2,128)(2,1)}, u32[]{:S(2)}) copy-start(bf16[512,2,128]{2,1,0:T(2,128)(2,1)} %reshape.119) | copy-start | bytes 786436
  149.7 36.2 %all-to-all-start.7 = ((bf16[4,128,256]{2,1,0:T(8,128)(2,1)}), bf16[4,128,256]{2,1,0:T(8,128)(2,1)}, u32[]{:S(2)}, u32[]{:S(2)}) async-start(bf16[4,128,256]{2,1,0:T(8,128)(2,1)} %all_to_all.120), calls=%async_computation.9 | async-start | bytes 524288 | tf_op jit(solution)/shard_map/all_to_all | solution.py:174
  186.0 16.8 %copy-start.12 = (bf16[512,2,4,128]{0,3,2,1:T(8,128)(2,1)S(1)}, bf16[512,2,4,128]{0,3,2,1:T(8,128)(2,1)}, u32[]{:S(2)}) copy-start(bf16[512,2,4,128]{0,3,2,1:T(8,128)(2,1)} %get-tuple-element.103) | copy-start | bytes 3145732
  186.0 13.2 %all-to-all-start.6 = ((bf16[4,128,256]{2,1,0:T(8,128)(2,1)}), bf16[4,128,256]{2,1,0:T(8,128)(2,1)}, u32[]{:S(2)}, u32[]{:S(2)}) async-start(bf16[4,128,256]{2,1,0:T(8,128)(2,1)} %all_to_all.116), calls=%async_computation.7 | async-start | bytes 524288 | tf_op jit(solution)/shard_map/all_to_all | solution.py:173
  199.2 27.7 %all-to-all-start.5 = ((bf16[4,128,1024]{2,1,0:T(8,128)(2,1)}), bf16[4,128,1024]{2,1,0:T(8,128)(2,1)S(1)}, u32[]{:S(2)}, u32[]{:S(2)}) async-start(bf16[4,128,1024]{2,1,0:T(8,128)(2,1)} %all_to_all.112), calls=%async_computation.5 | async-start | bytes 2097152 | tf_op jit(solution)/shard_map/all_to_all | solution.py:172
  226.9 28.7 %all-to-all-start.3 = ((bf16[4,128,1024]{1,2,0:T(8,128)(2,1)}), bf16[4,128,1024]{1,2,0:T(8,128)(2,1)S(1)}, u32[]{:S(2)}, u32[]{:S(2)}) async-start(bf16[4,128,1024]{1,2,0:T(8,128)(2,1)} %pad_maximum_fusion), calls=%async_computation.3 | async-start | bytes 2097152 | tf_op jit(solution)/shard_map/all_to_all | solution.py:167
  (4 other events, 14.1 us)
Sparse Core Ops, SparseCore 0:
  112.1 31.7 reduce-scatter.4
  147.7 33.5 reduce-scatter.2
